TPU v7x, 32 devices: a whole 2x2x4 slice. The times are simulated.
32 devices in a mesh: batch: 8 (over z, y), width: 4 (over x, core).
Axes of the slice: x: 2, y: 2, z: 4, core: 2. Of those that a mesh axis runs over, the one named last changes fastest.
Arguments:
- teacher: bfloat16 [2048, 4096], P('batch', 'width'), may hold values from -48 to 48, as said below
- student: bfloat16 [2048, 1024], P('batch', 'width'), may hold values from -48 to 48, as said below
Outputs:
- grad: float32 [2048, 1024], P('batch', 'width')
Inputs may be any that keep to these rules, and one draw needn't show every extreme that they name: `teacher`: Real-valued embeddings. `student`: Real-valued embeddings.
All inputs are finite; a program needn't handle non-finite values.
Results may differ from a plain program's by a relative error of at most 0.00075.
Values may be sent and summed in bfloat16 or wider, within the bound.
No kernel may reach another device: no remote copies, remote signals or barrier semaphores. Data moves between devices by JAX's collectives and lax.ppermute only.
A program may use at most 64 MiB of HBM per device.

v0:
```python
import jax
import jax.numpy as jnp
import numpy as np
from jax import lax
from jax.sharding import PartitionSpec as P

DT = 4096
DS = 1024
REACH = 4


def passed_along(block, axis, distance):
    devices = range(lax.axis_size(axis))
    route = [(i - distance, i) for i in devices if i - distance in devices]
    return lax.ppermute(block, axis, route)


def body(teacher, student):
    group = lax.axis_size("batch")
    owner = lax.axis_index("batch")
    rows_dev = teacher.shape[0]
    teacher_list = [teacher]
    student_list = [student]
    moving = (teacher, student)
    for offset in range(REACH):
        moving = passed_along((moving[0], moving[1]), "batch", -1)
        teacher_list.append(moving[0])
        student_list.append(moving[1])
    offset_list = list(range(REACH + 1))
    moving = (teacher, student)
    for offset in range(REACH):
        moving = passed_along((moving[0], moving[1]), "batch", 1)
        teacher_list.insert(0, moving[0])
        student_list.insert(0, moving[1])
        offset_list.insert(0, -(offset + 1))
    band_teacher = jnp.stack(teacher_list, axis=0)
    band_student = jnp.stack(student_list, axis=0)
    own_tsq = jnp.sum(jnp.square(teacher.astype(jnp.float32)), axis=1) / DT
    own_ssq = jnp.sum(jnp.square(student.astype(jnp.float32)), axis=1) / DS
    band_tsq = jnp.sum(jnp.square(band_teacher.astype(jnp.float32)), axis=2) / DT
    band_ssq = jnp.sum(jnp.square(band_student.astype(jnp.float32)), axis=2) / DS
    tgram = jnp.einsum("rk,wck->wrc", teacher, band_teacher, preferred_element_type=jnp.float32)
    sgram = jnp.einsum("rk,wck->wrc", student, band_student, preferred_element_type=jnp.float32)
    student_part = own_ssq[None, :, None] + band_ssq[:, None, :] - 2.0 * sgram / DS
    teacher_part = own_tsq[None, :, None] + band_tsq[:, None, :] - 2.0 * tgram / DT
    shard_terms = student_part - teacher_part
    partner = owner + jnp.asarray(np.array(offset_list, dtype=np.int32))
    valid = jnp.logical_and(partner >= 0, partner < group)
    residual = lax.psum(shard_terms, "width")
    residual = jnp.where(valid[:, None, None], residual, jnp.zeros_like(residual))
    residual_low = residual.astype(jnp.bfloat16)
    row_total = jnp.sum(residual, axis=(0, 2))
    pulled = jnp.einsum(
        "wrc,wck->rk", residual_low, band_student, preferred_element_type=jnp.float32
    )
    near_count = (2 * REACH + 1) * rows_dev
    grad = (student.astype(jnp.float32) * row_total[:, None] - pulled) / near_count
    return grad


def solution(mesh):
    in_specs = (P("batch", "width"), P("batch", "width"))
    out_specs = P("batch", "width")
    return jax.shard_map(body, mesh=mesh, in_specs=in_specs, out_specs=out_specs, check_vma=False)
```

profile of v0, /device:TPU:0, one launch (start us, length us, event | category | flops | bytes accessed | tf_op | source)
XLA Modules:
  0.0 210.9 jit_solution(6608622640676647879)
XLA Ops:
  6.5 5.0 %collective-permute-start = (bf16[256,256]{1,0:T(8,128)(2,1)}, bf16[256,256]{1,0:T(8,128)(2,1)S(1)}, u32[]{:S(2)}, u32[]{:S(2)}) collective-permute-start(bf16[256,256]{1,0:T(8,128)(2,1)} %param.4), channel_id=1, source_target_pairs={{0,4},{4,8},{8,12},{12,16},{16,20},{20,24},{24,28},{1,5},{5,9},{9,... | collective-permute-start | bytes 393224 | tf_op jit(solution)/shard_map/ppermute | solution.py:15
  11.6 1.3 collective-permute-start.4
  12.9 4.6 %collective-permute-start.8 = (bf16[256,1024]{1,0:T(8,128)(2,1)}, bf16[256,1024]{1,0:T(8,128)(2,1)S(1)}, u32[]{:S(2)}, u32[]{:S(2)}) collective-permute-start(bf16[256,1024]{1,0:T(8,128)(2,1)} %param.3), channel_id=1, source_target_pairs={{0,4},{4,8},{8,12},{12,16},{16,20},{20,24},{24,28},{1,5},{5,9},{9,... | collective-permute-start | bytes 1572872 | tf_op jit(solution)/shard_map/ppermute | solution.py:15
  17.5 1.3 collective-permute-start.12
  18.8 4.9 %collective-permute-start.1 = (bf16[256,256]{1,0:T(8,128)(2,1)S(1)}, bf16[256,256]{1,0:T(8,128)(2,1)S(1)}, u32[]{:S(2)}, u32[]{:S(2)}) collective-permute-start(bf16[256,256]{1,0:T(8,128)(2,1)S(1)} %collective-permute-done), channel_id=1, source_target_pairs={{0,4},{4,8},{8,12},{12,16},{16,20},{20,24},{24,28},{1,5},{5,9},{9,... | collective-permute-start | bytes 393224 | tf_op jit(solution)/shard_map/ppermute | solution.py:15
  23.7 1.2 multiply_reduce_fusion.2
  24.9 1.3 collective-permute-start.5
  26.2 20.4 %collective-permute-done.1 = bf16[256,256]{1,0:T(8,128)(2,1)S(1)} collective-permute-done((bf16[256,256]{1,0:T(8,128)(2,1)S(1)}, bf16[256,256]{1,0:T(8,128)(2,1)S(1)}, u32[]{:S(2)}, u32[]{:S(2)}) %collective-permute-start.1) | collective-permute-done | bytes 131104 | tf_op jit(solution)/shard_map/ppermute | solution.py:15
  46.7 4.4 %collective-permute-start.2 = (bf16[256,256]{1,0:T(8,128)(2,1)S(1)}, bf16[256,256]{1,0:T(8,128)(2,1)S(1)}, u32[]{:S(2)}, u32[]{:S(2)}) collective-permute-start(bf16[256,256]{1,0:T(8,128)(2,1)S(1)} %collective-permute-done.1), channel_id=1, source_target_pairs={{0,4},{4,8},{8,12},{12,16},{16,20},{20,24},{24,28},{1,5},{5,9},{9,... | collective-permute-start | bytes 393224 | tf_op jit(solution)/shard_map/ppermute | solution.py:15
  51.1 1.0 fusion.8
  52.1 1.3 collective-permute-start.6
  53.4 0.5 collective-permute-done.2
  53.9 4.4 %collective-permute-start.3 = (bf16[256,256]{1,0:T(8,128)(2,1)S(1)}, bf16[256,256]{1,0:T(8,128)(2,1)S(1)}, u32[]{:S(2)}, u32[]{:S(2)}) collective-permute-start(bf16[256,256]{1,0:T(8,128)(2,1)S(1)} %collective-permute-done.2), channel_id=1, source_target_pairs={{0,4},{4,8},{8,12},{12,16},{16,20},{20,24},{24,28},{1,5},{5,9},{9,... | collective-permute-start | bytes 393224 | tf_op jit(solution)/shard_map/ppermute | solution.py:15
  58.3 0.8 collective-permute-done.6
  59.1 1.3 collective-permute-start.7
  60.9 4.4 %collective-permute-start.9 = (bf16[256,1024]{1,0:T(8,128)(2,1)S(1)}, bf16[256,1024]{1,0:T(8,128)(2,1)S(1)}, u32[]{:S(2)}, u32[]{:S(2)}) collective-permute-start(bf16[256,1024]{1,0:T(8,128)(2,1)S(1)} %collective-permute-done.8), channel_id=1, source_target_pairs={{0,4},{4,8},{8,12},{12,16},{16,20},{20,24},{24,28},{1,5},{5,9},{9,... | collective-permute-start | bytes 1572872 | tf_op jit(solution)/shard_map/ppermute | solution.py:15
  65.4 0.9 bitcast_dynamic-update-slice_fusion.13
  66.3 1.3 collective-permute-start.13
  67.6 20.5 %collective-permute-done.9 = bf16[256,1024]{1,0:T(8,128)(2,1)S(1)} collective-permute-done((bf16[256,1024]{1,0:T(8,128)(2,1)S(1)}, bf16[256,1024]{1,0:T(8,128)(2,1)S(1)}, u32[]{:S(2)}, u32[]{:S(2)}) %collective-permute-start.9) | collective-permute-done | bytes 524320 | tf_op jit(solution)/shard_map/ppermute | solution.py:15
  88.1 4.4 %collective-permute-start.10 = (bf16[256,1024]{1,0:T(8,128)(2,1)S(1)}, bf16[256,1024]{1,0:T(8,128)(2,1)S(1)}, u32[]{:S(2)}, u32[]{:S(2)}) collective-permute-start(bf16[256,1024]{1,0:T(8,128)(2,1)S(1)} %collective-permute-done.9), channel_id=1, source_target_pairs={{0,4},{4,8},{8,12},{12,16},{16,20},{20,24},{24,28},{1,5},{5,9},{9,... | collective-permute-start | bytes 1572872 | tf_op jit(solution)/shard_map/ppermute | solution.py:15
  93.0 1.3 collective-permute-start.14
  94.3 20.1 %collective-permute-done.10 = bf16[256,1024]{1,0:T(8,128)(2,1)S(1)} collective-permute-done((bf16[256,1024]{1,0:T(8,128)(2,1)S(1)}, bf16[256,1024]{1,0:T(8,128)(2,1)S(1)}, u32[]{:S(2)}, u32[]{:S(2)}) %collective-permute-start.10) | collective-permute-done | bytes 524320 | tf_op jit(solution)/shard_map/ppermute | solution.py:15
  114.4 4.4 %collective-permute-start.11 = (bf16[256,1024]{1,0:T(8,128)(2,1)S(1)}, bf16[256,1024]{1,0:T(8,128)(2,1)S(1)}, u32[]{:S(2)}, u32[]{:S(2)}) collective-permute-start(bf16[256,1024]{1,0:T(8,128)(2,1)S(1)} %collective-permute-done.10), channel_id=1, source_target_pairs={{0,4},{4,8},{8,12},{12,16},{16,20},{20,24},{24,28},{1,5},{5,9},{9,... | collective-permute-start | bytes 1572872 | tf_op jit(solution)/shard_map/ppermute | solution.py:15
  118.8 0.5 fusion.9
  119.4 1.4 collective-permute-start.15
  120.8 19.0 %collective-permute-done.11 = bf16[256,1024]{1,0:T(8,128)(2,1)S(1)} collective-permute-done((bf16[256,1024]{1,0:T(8,128)(2,1)S(1)}, bf16[256,1024]{1,0:T(8,128)(2,1)S(1)}, u32[]{:S(2)}, u32[]{:S(2)}) %collective-permute-start.11) | collective-permute-done | bytes 524320 | tf_op jit(solution)/shard_map/ppermute | solution.py:15
  140.3 1.0 multiply_reduce_fusion
  141.3 3.0 %fusion = f32[9,256,256]{1,2,0:T(8,128)} fusion(f32[9,256,256]{2,1,0:T(8,128)S(1)} %fusion.9, bf16[9,256,1024]{2,1,0:T(8,128)(2,1)S(1)} %bitcast_dynamic-update-slice_fusion, f32[9,256]{1,0:T(8,128)S(1)} %broadcast_multiply_fusion, f32[256]{0:T(256)S(1)} %broadcast_multiply_fusion.2, f32[9,256]{1,0:T(8,128)S(1)} %broadcast_multiply_fusion.1, ...), kind=kOutput, calls=%fused_computation.2 | convolution fusion | flops 1212088320 | bytes 9981952 | tf_op jit(solution)/shard_map/rk,wck->wrc/dot_general | solution.py:42
  144.3 0.6 copy-done.3
  144.9 55.3 %all-reduce.2.cloned.1.call-done = f32[9,256,256]{1,2,0:T(8,128)} async-done(((f32[9,256,256]{1,2,0:T(8,128)}), f32[9,256,256]{1,2,0:T(8,128)}) %all-reduce.2.cloned.1.call-update) | async-done | bytes 2359312 | tf_op jit(solution)/shard_map/psum | solution.py:49
  200.3 2.2 %select_reduce_fusion = f32[256]{0:T(256)S(1)} fusion(f32[9,256,256]{1,2,0:T(8,128)} %all-reduce.2.cloned.1.call-done, pred[9]{0:T(512)(128)(4,1)S(1)} %compare_and_fusion), kind=kLoop, calls=%fused_computation.6 | loop fusion | flops 1179392 | bytes 2360329 | tf_op jit(solution)/shard_map/reduce_sum | solution.py:52
  202.7 1.4 fusion.6
  (42 shorter events, 1.5 us)
Async XLA Ops:
  6.5 112.3 %copy-start.1 = (bf16[256,256]{1,0:T(8,128)(2,1)S(1)}, bf16[256,256]{1,0:T(8,128)(2,1)}, u32[]{:S(2)}) copy-start(bf16[256,256]{1,0:T(8,128)(2,1)} %param.4) | copy-start | bytes 393220
  6.5 193.7 %all-reduce.2.cloned.1.call-start = ((), (), s32[]{:S(2)}) async-start(), calls=%async_computation | async-start | bytes 4718592 | tf_op jit(solution)/shard_map/psum | solution.py:49
  6.5 12.2 %collective-permute-start = (bf16[256,256]{1,0:T(8,128)(2,1)}, bf16[256,256]{1,0:T(8,128)(2,1)S(1)}, u32[]{:S(2)}, u32[]{:S(2)}) collective-permute-start(bf16[256,256]{1,0:T(8,128)(2,1)} %param.4), channel_id=1, source_target_pairs={{0,4},{4,8},{8,12},{12,16},{16,20},{20,24},{24,28},{1,5},{5,9},{9,... | collective-permute-start | bytes 393224 | tf_op jit(solution)/shard_map/ppermute | solution.py:15
  11.6 13.4 %collective-permute-start.4 = (bf16[256,256]{1,0:T(8,128)(2,1)}, bf16[256,256]{1,0:T(8,128)(2,1)S(1)}, u32[]{:S(2)}, u32[]{:S(2)}) collective-permute-start(bf16[256,256]{1,0:T(8,128)(2,1)} %param.4), channel_id=1, source_target_pairs={{4,0},{8,4},{12,8},{16,12},{20,16},{24,20},{28,24},{5,1},{9,5},{13... | collective-permute-start | bytes 393224 | tf_op jit(solution)/shard_map/ppermute | solution.py:15
  12.9 48.0 %collective-permute-start.8 = (bf16[256,1024]{1,0:T(8,128)(2,1)}, bf16[256,1024]{1,0:T(8,128)(2,1)S(1)}, u32[]{:S(2)}, u32[]{:S(2)}) collective-permute-start(bf16[256,1024]{1,0:T(8,128)(2,1)} %param.3), channel_id=1, source_target_pairs={{0,4},{4,8},{8,12},{12,16},{16,20},{20,24},{24,28},{1,5},{5,9},{9,... | collective-permute-start | bytes 1572872 | tf_op jit(solution)/shard_map/ppermute | solution.py:15
  17.5 48.8 %collective-permute-start.12 = (bf16[256,1024]{1,0:T(8,128)(2,1)}, bf16[256,1024]{1,0:T(8,128)(2,1)S(1)}, u32[]{:S(2)}, u32[]{:S(2)}) collective-permute-start(bf16[256,1024]{1,0:T(8,128)(2,1)} %param.3), channel_id=1, source_target_pairs={{4,0},{8,4},{12,8},{16,12},{20,16},{24,20},{28,24},{5,1},{9,5},{13... | collective-permute-start | bytes 1572872 | tf_op jit(solution)/shard_map/ppermute | solution.py:15
  18.8 27.9 %collective-permute-start.1 = (bf16[256,256]{1,0:T(8,128)(2,1)S(1)}, bf16[256,256]{1,0:T(8,128)(2,1)S(1)}, u32[]{:S(2)}, u32[]{:S(2)}) collective-permute-start(bf16[256,256]{1,0:T(8,128)(2,1)S(1)} %collective-permute-done), channel_id=1, source_target_pairs={{0,4},{4,8},{8,12},{12,16},{16,20},{20,24},{24,28},{1,5},{5,9},{9,... | collective-permute-start | bytes 393224 | tf_op jit(solution)/shard_map/ppermute | solution.py:15
  24.9 27.1 %collective-permute-start.5 = (bf16[256,256]{1,0:T(8,128)(2,1)S(1)}, bf16[256,256]{1,0:T(8,128)(2,1)S(1)}, u32[]{:S(2)}, u32[]{:S(2)}) collective-permute-start(bf16[256,256]{1,0:T(8,128)(2,1)S(1)} %collective-permute-done.4), channel_id=1, source_target_pairs={{4,0},{8,4},{12,8},{16,12},{20,16},{24,20},{28,24},{5,1},{9,5},{13... | collective-permute-start | bytes 393224 | tf_op jit(solution)/shard_map/ppermute | solution.py:15
  46.7 7.3 %collective-permute-start.2 = (bf16[256,256]{1,0:T(8,128)(2,1)S(1)}, bf16[256,256]{1,0:T(8,128)(2,1)S(1)}, u32[]{:S(2)}, u32[]{:S(2)}) collective-permute-start(bf16[256,256]{1,0:T(8,128)(2,1)S(1)} %collective-permute-done.1), channel_id=1, source_target_pairs={{0,4},{4,8},{8,12},{12,16},{16,20},{20,24},{24,28},{1,5},{5,9},{9,... | collective-permute-start | bytes 393224 | tf_op jit(solution)/shard_map/ppermute | solution.py:15
  52.1 7.0 %collective-permute-start.6 = (bf16[256,256]{1,0:T(8,128)(2,1)S(1)}, bf16[256,256]{1,0:T(8,128)(2,1)S(1)}, u32[]{:S(2)}, u32[]{:S(2)}) collective-permute-start(bf16[256,256]{1,0:T(8,128)(2,1)S(1)} %collective-permute-done.5), channel_id=1, source_target_pairs={{4,0},{8,4},{12,8},{16,12},{20,16},{24,20},{28,24},{5,1},{9,5},{13... | collective-permute-start | bytes 393224 | tf_op jit(solution)/shard_map/ppermute | solution.py:15
  53.9 6.9 %collective-permute-start.3 = (bf16[256,256]{1,0:T(8,128)(2,1)S(1)}, bf16[256,256]{1,0:T(8,128)(2,1)S(1)}, u32[]{:S(2)}, u32[]{:S(2)}) collective-permute-start(bf16[256,256]{1,0:T(8,128)(2,1)S(1)} %collective-permute-done.2), channel_id=1, source_target_pairs={{0,4},{4,8},{8,12},{12,16},{16,20},{20,24},{24,28},{1,5},{5,9},{9,... | collective-permute-start | bytes 393224 | tf_op jit(solution)/shard_map/ppermute | solution.py:15
  59.1 33.4 %collective-permute-start.7 = (bf16[256,256]{1,0:T(8,128)(2,1)S(1)}, bf16[256,256]{1,0:T(8,128)(2,1)S(1)}, u32[]{:S(2)}, u32[]{:S(2)}) collective-permute-start(bf16[256,256]{1,0:T(8,128)(2,1)S(1)} %collective-permute-done.6), channel_id=1, source_target_pairs={{4,0},{8,4},{12,8},{16,12},{20,16},{24,20},{28,24},{5,1},{9,5},{13... | collective-permute-start | bytes 393224 | tf_op jit(solution)/shard_map/ppermute | solution.py:15
  60.9 27.2 %collective-permute-start.9 = (bf16[256,1024]{1,0:T(8,128)(2,1)S(1)}, bf16[256,1024]{1,0:T(8,128)(2,1)S(1)}, u32[]{:S(2)}, u32[]{:S(2)}) collective-permute-start(bf16[256,1024]{1,0:T(8,128)(2,1)S(1)} %collective-permute-done.8), channel_id=1, source_target_pairs={{0,4},{4,8},{8,12},{12,16},{16,20},{20,24},{24,28},{1,5},{5,9},{9,... | collective-permute-start | bytes 1572872 | tf_op jit(solution)/shard_map/ppermute | solution.py:15
  66.3 26.6 %collective-permute-start.13 = (bf16[256,1024]{1,0:T(8,128)(2,1)S(1)}, bf16[256,1024]{1,0:T(8,128)(2,1)S(1)}, u32[]{:S(2)}, u32[]{:S(2)}) collective-permute-start(bf16[256,1024]{1,0:T(8,128)(2,1)S(1)} %collective-permute-done.12), channel_id=1, source_target_pairs={{4,0},{8,4},{12,8},{16,12},{20,16},{24,20},{28,24},{5,1},{9,5},{13... | collective-permute-start | bytes 1572872 | tf_op jit(solution)/shard_map/ppermute | solution.py:15
  88.1 26.3 %collective-permute-start.10 = (bf16[256,1024]{1,0:T(8,128)(2,1)S(1)}, bf16[256,1024]{1,0:T(8,128)(2,1)S(1)}, u32[]{:S(2)}, u32[]{:S(2)}) collective-permute-start(bf16[256,1024]{1,0:T(8,128)(2,1)S(1)} %collective-permute-done.9), channel_id=1, source_target_pairs={{0,4},{4,8},{8,12},{12,16},{16,20},{20,24},{24,28},{1,5},{5,9},{9,... | collective-permute-start | bytes 1572872 | tf_op jit(solution)/shard_map/ppermute | solution.py:15
  93.0 26.4 %collective-permute-start.14 = (bf16[256,1024]{1,0:T(8,128)(2,1)S(1)}, bf16[256,1024]{1,0:T(8,128)(2,1)S(1)}, u32[]{:S(2)}, u32[]{:S(2)}) collective-permute-start(bf16[256,1024]{1,0:T(8,128)(2,1)S(1)} %collective-permute-done.13), channel_id=1, source_target_pairs={{4,0},{8,4},{12,8},{16,12},{20,16},{24,20},{28,24},{5,1},{9,5},{13... | collective-permute-start | bytes 1572872 | tf_op jit(solution)/shard_map/ppermute | solution.py:15
  114.4 25.4 %collective-permute-start.11 = (bf16[256,1024]{1,0:T(8,128)(2,1)S(1)}, bf16[256,1024]{1,0:T(8,128)(2,1)S(1)}, u32[]{:S(2)}, u32[]{:S(2)}) collective-permute-start(bf16[256,1024]{1,0:T(8,128)(2,1)S(1)} %collective-permute-done.10), channel_id=1, source_target_pairs={{0,4},{4,8},{8,12},{12,16},{16,20},{20,24},{24,28},{1,5},{5,9},{9,... | collective-permute-start | bytes 1572872 | tf_op jit(solution)/shard_map/ppermute | solution.py:15
  119.3 20.7 %copy-start.2 = (bf16[256,1024]{1,0:T(8,128)(2,1)S(1)}, bf16[256,1024]{1,0:T(8,128)(2,1)}, u32[]{:S(2)}) copy-start(bf16[256,1024]{1,0:T(8,128)(2,1)} %param.3) | copy-start | bytes 1572868
  119.4 20.8 %collective-permute-start.15 = (bf16[256,1024]{1,0:T(8,128)(2,1)S(1)}, bf16[256,1024]{1,0:T(8,128)(2,1)S(1)}, u32[]{:S(2)}, u32[]{:S(2)}) collective-permute-start(bf16[256,1024]{1,0:T(8,128)(2,1)S(1)} %collective-permute-done.14), channel_id=1, source_target_pairs={{4,0},{8,4},{12,8},{16,12},{20,16},{24,20},{28,24},{5,1},{9,5},{13... | collective-permute-start | bytes 1572872 | tf_op jit(solution)/shard_map/ppermute | solution.py:15
  144.3 0.7 copy-start.3
  200.3 2.4 %copy-start = (f32[9,256,256]{1,2,0:T(8,128)S(1)}, f32[9,256,256]{1,2,0:T(8,128)}, u32[]{:S(2)}) copy-start(f32[9,256,256]{1,2,0:T(8,128)} %all-reduce.2.cloned.1.call-done) | copy-start | bytes 7077892
Sparse Core Ops, SparseCore 0:
  144.4 55.8 all-reduce.1
where the time goes:
time: 212 us; the launch traced here: 211 us
  waiting for transfers between devices  137 us (65%)
  starting transfers between devices  47 us (22%)
  between operations  13.8 us (7%)
  other arithmetic  5.87 us (3%)
  matrix products  4.92 us (2%)
    ppermute x16, waiting for transfers between devices, passed_along(): return lax.ppermute(block, axis, route)  81.9 us
    psum x1, waiting for transfers between devices, body(): residual = lax.psum(shard_terms, 'width')  55.3 us
    ppermute x16, starting transfers between devices, passed_along(): return lax.ppermute(block, axis, route)  47 us
  transfers between devices with their start and end apart: 17, of which 8 were waited for; matrix products, arithmetic and copies ran while one was open for 2% of the time, Pallas kernels for 0%

commit v1 on v0

--- a/solution.py
+++ b/solution.py
@@ -46,7 +46,7 @@
     shard_terms = student_part - teacher_part
     partner = owner + jnp.asarray(np.array(offset_list, dtype=np.int32))
     valid = jnp.logical_and(partner >= 0, partner < group)
-    residual = lax.psum(shard_terms, "width")
+    residual = jnp.sum(lax.all_gather(shard_terms, "width"), axis=0)
     residual = jnp.where(valid[:, None, None], residual, jnp.zeros_like(residual))
     residual_low = residual.astype(jnp.bfloat16)
     row_total = jnp.sum(residual, axis=(0, 2))

time: 212 us -> 228 us (1.075)
  waiting for transfers between devices: 137 us -> 146 us
  local copies, waits for them, and re-layouts: 2.1 us -> 6.43 us
  other arithmetic: 5.87 us -> 10.1 us
    all_gather x0 -> x1, waiting for transfers between devices: none -> 63.9 us  [body(): residual = jnp.sum(lax.all_gather(shard_terms, 'width'), axis=0)]
    psum x1 -> x0, waiting for transfers between devices: 55.3 us -> none  [body(): residual = lax.psum(shard_terms, 'width')]
    reduce_sum x0 -> x1, other arithmetic: none -> 6.02 us  [body(): residual = jnp.sum(lax.all_gather(shard_terms, 'width'), axis=0)]
    unnamed x24 -> x25, local copies, waits for them, and re-layouts: 2.06 us -> 4.43 us
where the time goes in v1:
time: 228 us; the launch traced here: 227 us
  waiting for transfers between devices  146 us (64%)
  starting transfers between devices  47 us (21%)
  between operations  13.8 us (6%)
  other arithmetic  10.1 us (4%)
  local copies, waits for them, and re-layouts  6.43 us (3%)
  matrix products  3.77 us (2%)
    ppermute x16, waiting for transfers between devices, passed_along(): return lax.ppermute(block, axis, route)  81.9 us
    all_gather x1, waiting for transfers between devices, body(): residual = jnp.sum(lax.all_gather(shard_terms, 'width'), axis=0)  63.9 us
    ppermute x16, starting transfers between devices, passed_along(): return lax.ppermute(block, axis, route)  47 us
    reduce_sum x1, other arithmetic, body(): residual = jnp.sum(lax.all_gather(shard_terms, 'width'), axis=0)  6.02 us
  transfers between devices with their start and end apart: 17, of which 8 were waited for; matrix products, arithmetic and copies ran while one was open for 2% of the time, Pallas kernels for 0%

profile of v1, /device:TPU:0, one launch (start us, length us, event | category | flops | bytes accessed | tf_op | source)
XLA Modules:
  0.0 226.9 jit_solution(7924033871963452263)
XLA Ops:
  6.5 5.0 %collective-permute-start = (bf16[256,256]{1,0:T(8,128)(2,1)}, bf16[256,256]{1,0:T(8,128)(2,1)S(1)}, u32[]{:S(2)}, u32[]{:S(2)}) collective-permute-start(bf16[256,256]{1,0:T(8,128)(2,1)} %param.4), channel_id=1, source_target_pairs={{0,4},{4,8},{8,12},{12,16},{16,20},{20,24},{24,28},{1,5},{5,9},{9,... | collective-permute-start | bytes 393224 | tf_op jit(solution)/shard_map/ppermute | solution.py:15
  11.6 1.3 collective-permute-start.4
  12.9 4.6 %collective-permute-start.8 = (bf16[256,1024]{1,0:T(8,128)(2,1)}, bf16[256,1024]{1,0:T(8,128)(2,1)S(1)}, u32[]{:S(2)}, u32[]{:S(2)}) collective-permute-start(bf16[256,1024]{1,0:T(8,128)(2,1)} %param.3), channel_id=1, source_target_pairs={{0,4},{4,8},{8,12},{12,16},{16,20},{20,24},{24,28},{1,5},{5,9},{9,... | collective-permute-start | bytes 1572872 | tf_op jit(solution)/shard_map/ppermute | solution.py:15
  17.5 1.3 collective-permute-start.12
  18.8 4.9 %collective-permute-start.1 = (bf16[256,256]{1,0:T(8,128)(2,1)S(1)}, bf16[256,256]{1,0:T(8,128)(2,1)S(1)}, u32[]{:S(2)}, u32[]{:S(2)}) collective-permute-start(bf16[256,256]{1,0:T(8,128)(2,1)S(1)} %collective-permute-done), channel_id=1, source_target_pairs={{0,4},{4,8},{8,12},{12,16},{16,20},{20,24},{24,28},{1,5},{5,9},{9,... | collective-permute-start | bytes 393224 | tf_op jit(solution)/shard_map/ppermute | solution.py:15
  23.7 1.2 multiply_reduce_fusion.2
  24.9 1.3 collective-permute-start.5
  26.2 20.4 %collective-permute-done.1 = bf16[256,256]{1,0:T(8,128)(2,1)S(1)} collective-permute-done((bf16[256,256]{1,0:T(8,128)(2,1)S(1)}, bf16[256,256]{1,0:T(8,128)(2,1)S(1)}, u32[]{:S(2)}, u32[]{:S(2)}) %collective-permute-start.1) | collective-permute-done | bytes 131104 | tf_op jit(solution)/shard_map/ppermute | solution.py:15
  46.7 4.4 %collective-permute-start.2 = (bf16[256,256]{1,0:T(8,128)(2,1)S(1)}, bf16[256,256]{1,0:T(8,128)(2,1)S(1)}, u32[]{:S(2)}, u32[]{:S(2)}) collective-permute-start(bf16[256,256]{1,0:T(8,128)(2,1)S(1)} %collective-permute-done.1), channel_id=1, source_target_pairs={{0,4},{4,8},{8,12},{12,16},{16,20},{20,24},{24,28},{1,5},{5,9},{9,... | collective-permute-start | bytes 393224 | tf_op jit(solution)/shard_map/ppermute | solution.py:15
  51.1 1.0 fusion.8
  52.1 1.3 collective-permute-start.6
  53.9 4.4 %collective-permute-start.3 = (bf16[256,256]{1,0:T(8,128)(2,1)S(1)}, bf16[256,256]{1,0:T(8,128)(2,1)S(1)}, u32[]{:S(2)}, u32[]{:S(2)}) collective-permute-start(bf16[256,256]{1,0:T(8,128)(2,1)S(1)} %collective-permute-done.2), channel_id=1, source_target_pairs={{0,4},{4,8},{8,12},{12,16},{16,20},{20,24},{24,28},{1,5},{5,9},{9,... | collective-permute-start | bytes 393224 | tf_op jit(solution)/shard_map/ppermute | solution.py:15
  58.3 0.8 collective-permute-done.6
  59.1 1.3 collective-permute-start.7
  60.9 4.4 %collective-permute-start.9 = (bf16[256,1024]{1,0:T(8,128)(2,1)S(1)}, bf16[256,1024]{1,0:T(8,128)(2,1)S(1)}, u32[]{:S(2)}, u32[]{:S(2)}) collective-permute-start(bf16[256,1024]{1,0:T(8,128)(2,1)S(1)} %collective-permute-done.8), channel_id=1, source_target_pairs={{0,4},{4,8},{8,12},{12,16},{16,20},{20,24},{24,28},{1,5},{5,9},{9,... | collective-permute-start | bytes 1572872 | tf_op jit(solution)/shard_map/ppermute | solution.py:15
  65.4 0.9 bitcast_dynamic-update-slice_fusion.13
  66.3 1.3 collective-permute-start.13
  67.6 20.5 %collective-permute-done.9 = bf16[256,1024]{1,0:T(8,128)(2,1)S(1)} collective-permute-done((bf16[256,1024]{1,0:T(8,128)(2,1)S(1)}, bf16[256,1024]{1,0:T(8,128)(2,1)S(1)}, u32[]{:S(2)}, u32[]{:S(2)}) %collective-permute-start.9) | collective-permute-done | bytes 524320 | tf_op jit(solution)/shard_map/ppermute | solution.py:15
  88.1 4.4 %collective-permute-start.10 = (bf16[256,1024]{1,0:T(8,128)(2,1)S(1)}, bf16[256,1024]{1,0:T(8,128)(2,1)S(1)}, u32[]{:S(2)}, u32[]{:S(2)}) collective-permute-start(bf16[256,1024]{1,0:T(8,128)(2,1)S(1)} %collective-permute-done.9), channel_id=1, source_target_pairs={{0,4},{4,8},{8,12},{12,16},{16,20},{20,24},{24,28},{1,5},{5,9},{9,... | collective-permute-start | bytes 1572872 | tf_op jit(solution)/shard_map/ppermute | solution.py:15
  93.0 1.3 collective-permute-start.14
  94.3 20.1 %collective-permute-done.10 = bf16[256,1024]{1,0:T(8,128)(2,1)S(1)} collective-permute-done((bf16[256,1024]{1,0:T(8,128)(2,1)S(1)}, bf16[256,1024]{1,0:T(8,128)(2,1)S(1)}, u32[]{:S(2)}, u32[]{:S(2)}) %collective-permute-start.10) | collective-permute-done | bytes 524320 | tf_op jit(solution)/shard_map/ppermute | solution.py:15
  114.4 4.4 %collective-permute-start.11 = (bf16[256,1024]{1,0:T(8,128)(2,1)S(1)}, bf16[256,1024]{1,0:T(8,128)(2,1)S(1)}, u32[]{:S(2)}, u32[]{:S(2)}) collective-permute-start(bf16[256,1024]{1,0:T(8,128)(2,1)S(1)} %collective-permute-done.10), channel_id=1, source_target_pairs={{0,4},{4,8},{8,12},{12,16},{16,20},{20,24},{24,28},{1,5},{5,9},{9,... | collective-permute-start | bytes 1572872 | tf_op jit(solution)/shard_map/ppermute | solution.py:15
  119.4 1.4 collective-permute-start.15
  120.8 19.0 %collective-permute-done.11 = bf16[256,1024]{1,0:T(8,128)(2,1)S(1)} collective-permute-done((bf16[256,1024]{1,0:T(8,128)(2,1)S(1)}, bf16[256,1024]{1,0:T(8,128)(2,1)S(1)}, u32[]{:S(2)}, u32[]{:S(2)}) %collective-permute-start.11) | collective-permute-done | bytes 524320 | tf_op jit(solution)/shard_map/ppermute | solution.py:15
  140.3 1.0 multiply_reduce_fusion
  141.3 1.9 fusion
  143.1 1.9 copy.4
  145.1 0.6 copy-done.3
  145.8 63.9 %all-gather.3.cloned.1.call-done = f32[36,256,256]{2,1,0:T(8,128)} async-done(((f32[9,256,256]{2,1,0:T(8,128)}), f32[36,256,256]{2,1,0:T(8,128)}) %all-gather.3.cloned.1.call-update) | async-done | bytes 9437200 | tf_op jit(solution)/shard_map/all_gather | solution.py:49
  209.7 6.0 %reduce_sum.58 = f32[9,256,256]{2,1,0:T(8,128)} reduce(f32[4,9,256,256]{3,2,1,0:T(8,128)} %bitcast.60, f32[]{:T(128)} %constant.31.clone.1), dimensions={0}, to_apply=%region_4.0 | reduce | flops 1769472 | bytes 11796484 | tf_op jit(solution)/shard_map/reduce_sum | solution.py:49
  215.7 2.0 copy.8
  218.6 1.4 fusion.6
  (45 shorter events, 3.3 us)
Async XLA Ops:
  6.5 112.3 %copy-start = (bf16[256,256]{1,0:T(8,128)(2,1)S(1)}, bf16[256,256]{1,0:T(8,128)(2,1)}, u32[]{:S(2)}) copy-start(bf16[256,256]{1,0:T(8,128)(2,1)} %param.4) | copy-start | bytes 393220
  6.5 203.1 %all-gather.3.cloned.1.call-start = ((), (), s32[]{:S(2)}) async-start(), calls=%async_computation | async-start | bytes 11796480 | tf_op jit(solution)/shard_map/all_gather | solution.py:49
  6.5 12.2 %collective-permute-start = (bf16[256,256]{1,0:T(8,128)(2,1)}, bf16[256,256]{1,0:T(8,128)(2,1)S(1)}, u32[]{:S(2)}, u32[]{:S(2)}) collective-permute-start(bf16[256,256]{1,0:T(8,128)(2,1)} %param.4), channel_id=1, source_target_pairs={{0,4},{4,8},{8,12},{12,16},{16,20},{20,24},{24,28},{1,5},{5,9},{9,... | collective-permute-start | bytes 393224 | tf_op jit(solution)/shard_map/ppermute | solution.py:15
  11.6 13.4 %collective-permute-start.4 = (bf16[256,256]{1,0:T(8,128)(2,1)}, bf16[256,256]{1,0:T(8,128)(2,1)S(1)}, u32[]{:S(2)}, u32[]{:S(2)}) collective-permute-start(bf16[256,256]{1,0:T(8,128)(2,1)} %param.4), channel_id=1, source_target_pairs={{4,0},{8,4},{12,8},{16,12},{20,16},{24,20},{28,24},{5,1},{9,5},{13... | collective-permute-start | bytes 393224 | tf_op jit(solution)/shard_map/ppermute | solution.py:15
  12.9 48.0 %collective-permute-start.8 = (bf16[256,1024]{1,0:T(8,128)(2,1)}, bf16[256,1024]{1,0:T(8,128)(2,1)S(1)}, u32[]{:S(2)}, u32[]{:S(2)}) collective-permute-start(bf16[256,1024]{1,0:T(8,128)(2,1)} %param.3), channel_id=1, source_target_pairs={{0,4},{4,8},{8,12},{12,16},{16,20},{20,24},{24,28},{1,5},{5,9},{9,... | collective-permute-start | bytes 1572872 | tf_op jit(solution)/shard_map/ppermute | solution.py:15
  17.5 48.8 %collective-permute-start.12 = (bf16[256,1024]{1,0:T(8,128)(2,1)}, bf16[256,1024]{1,0:T(8,128)(2,1)S(1)}, u32[]{:S(2)}, u32[]{:S(2)}) collective-permute-start(bf16[256,1024]{1,0:T(8,128)(2,1)} %param.3), channel_id=1, source_target_pairs={{4,0},{8,4},{12,8},{16,12},{20,16},{24,20},{28,24},{5,1},{9,5},{13... | collective-permute-start | bytes 1572872 | tf_op jit(solution)/shard_map/ppermute | solution.py:15
  18.8 27.9 %collective-permute-start.1 = (bf16[256,256]{1,0:T(8,128)(2,1)S(1)}, bf16[256,256]{1,0:T(8,128)(2,1)S(1)}, u32[]{:S(2)}, u32[]{:S(2)}) collective-permute-start(bf16[256,256]{1,0:T(8,128)(2,1)S(1)} %collective-permute-done), channel_id=1, source_target_pairs={{0,4},{4,8},{8,12},{12,16},{16,20},{20,24},{24,28},{1,5},{5,9},{9,... | collective-permute-start | bytes 393224 | tf_op jit(solution)/shard_map/ppermute | solution.py:15
  24.9 27.1 %collective-permute-start.5 = (bf16[256,256]{1,0:T(8,128)(2,1)S(1)}, bf16[256,256]{1,0:T(8,128)(2,1)S(1)}, u32[]{:S(2)}, u32[]{:S(2)}) collective-permute-start(bf16[256,256]{1,0:T(8,128)(2,1)S(1)} %collective-permute-done.4), channel_id=1, source_target_pairs={{4,0},{8,4},{12,8},{16,12},{20,16},{24,20},{28,24},{5,1},{9,5},{13... | collective-permute-start | bytes 393224 | tf_op jit(solution)/shard_map/ppermute | solution.py:15
  46.7 7.3 %collective-permute-start.2 = (bf16[256,256]{1,0:T(8,128)(2,1)S(1)}, bf16[256,256]{1,0:T(8,128)(2,1)S(1)}, u32[]{:S(2)}, u32[]{:S(2)}) collective-permute-start(bf16[256,256]{1,0:T(8,128)(2,1)S(1)} %collective-permute-done.1), channel_id=1, source_target_pairs={{0,4},{4,8},{8,12},{12,16},{16,20},{20,24},{24,28},{1,5},{5,9},{9,... | collective-permute-start | bytes 393224 | tf_op jit(solution)/shard_map/ppermute | solution.py:15
  52.1 7.0 %collective-permute-start.6 = (bf16[256,256]{1,0:T(8,128)(2,1)S(1)}, bf16[256,256]{1,0:T(8,128)(2,1)S(1)}, u32[]{:S(2)}, u32[]{:S(2)}) collective-permute-start(bf16[256,256]{1,0:T(8,128)(2,1)S(1)} %collective-permute-done.5), channel_id=1, source_target_pairs={{4,0},{8,4},{12,8},{16,12},{20,16},{24,20},{28,24},{5,1},{9,5},{13... | collective-permute-start | bytes 393224 | tf_op jit(solution)/shard_map/ppermute | solution.py:15
  53.9 6.9 %collective-permute-start.3 = (bf16[256,256]{1,0:T(8,128)(2,1)S(1)}, bf16[256,256]{1,0:T(8,128)(2,1)S(1)}, u32[]{:S(2)}, u32[]{:S(2)}) collective-permute-start(bf16[256,256]{1,0:T(8,128)(2,1)S(1)} %collective-permute-done.2), channel_id=1, source_target_pairs={{0,4},{4,8},{8,12},{12,16},{16,20},{20,24},{24,28},{1,5},{5,9},{9,... | collective-permute-start | bytes 393224 | tf_op jit(solution)/shard_map/ppermute | solution.py:15
  59.1 33.4 %collective-permute-start.7 = (bf16[256,256]{1,0:T(8,128)(2,1)S(1)}, bf16[256,256]{1,0:T(8,128)(2,1)S(1)}, u32[]{:S(2)}, u32[]{:S(2)}) collective-permute-start(bf16[256,256]{1,0:T(8,128)(2,1)S(1)} %collective-permute-done.6), channel_id=1, source_target_pairs={{4,0},{8,4},{12,8},{16,12},{20,16},{24,20},{28,24},{5,1},{9,5},{13... | collective-permute-start | bytes 393224 | tf_op jit(solution)/shard_map/ppermute | solution.py:15
  60.9 27.2 %collective-permute-start.9 = (bf16[256,1024]{1,0:T(8,128)(2,1)S(1)}, bf16[256,1024]{1,0:T(8,128)(2,1)S(1)}, u32[]{:S(2)}, u32[]{:S(2)}) collective-permute-start(bf16[256,1024]{1,0:T(8,128)(2,1)S(1)} %collective-permute-done.8), channel_id=1, source_target_pairs={{0,4},{4,8},{8,12},{12,16},{16,20},{20,24},{24,28},{1,5},{5,9},{9,... | collective-permute-start | bytes 1572872 | tf_op jit(solution)/shard_map/ppermute | solution.py:15
  66.3 26.6 %collective-permute-start.13 = (bf16[256,1024]{1,0:T(8,128)(2,1)S(1)}, bf16[256,1024]{1,0:T(8,128)(2,1)S(1)}, u32[]{:S(2)}, u32[]{:S(2)}) collective-permute-start(bf16[256,1024]{1,0:T(8,128)(2,1)S(1)} %collective-permute-done.12), channel_id=1, source_target_pairs={{4,0},{8,4},{12,8},{16,12},{20,16},{24,20},{28,24},{5,1},{9,5},{13... | collective-permute-start | bytes 1572872 | tf_op jit(solution)/shard_map/ppermute | solution.py:15
  88.1 26.3 %collective-permute-start.10 = (bf16[256,1024]{1,0:T(8,128)(2,1)S(1)}, bf16[256,1024]{1,0:T(8,128)(2,1)S(1)}, u32[]{:S(2)}, u32[]{:S(2)}) collective-permute-start(bf16[256,1024]{1,0:T(8,128)(2,1)S(1)} %collective-permute-done.9), channel_id=1, source_target_pairs={{0,4},{4,8},{8,12},{12,16},{16,20},{20,24},{24,28},{1,5},{5,9},{9,... | collective-permute-start | bytes 1572872 | tf_op jit(solution)/shard_map/ppermute | solution.py:15
  93.0 26.4 %collective-permute-start.14 = (bf16[256,1024]{1,0:T(8,128)(2,1)S(1)}, bf16[256,1024]{1,0:T(8,128)(2,1)S(1)}, u32[]{:S(2)}, u32[]{:S(2)}) collective-permute-start(bf16[256,1024]{1,0:T(8,128)(2,1)S(1)} %collective-permute-done.13), channel_id=1, source_target_pairs={{4,0},{8,4},{12,8},{16,12},{20,16},{24,20},{28,24},{5,1},{9,5},{13... | collective-permute-start | bytes 1572872 | tf_op jit(solution)/shard_map/ppermute | solution.py:15
  114.4 25.4 %collective-permute-start.11 = (bf16[256,1024]{1,0:T(8,128)(2,1)S(1)}, bf16[256,1024]{1,0:T(8,128)(2,1)S(1)}, u32[]{:S(2)}, u32[]{:S(2)}) collective-permute-start(bf16[256,1024]{1,0:T(8,128)(2,1)S(1)} %collective-permute-done.10), channel_id=1, source_target_pairs={{0,4},{4,8},{8,12},{12,16},{16,20},{20,24},{24,28},{1,5},{5,9},{9,... | collective-permute-start | bytes 1572872 | tf_op jit(solution)/shard_map/ppermute | solution.py:15
  119.3 20.7 %copy-start.2 = (bf16[256,1024]{1,0:T(8,128)(2,1)S(1)}, bf16[256,1024]{1,0:T(8,128)(2,1)}, u32[]{:S(2)}) copy-start(bf16[256,1024]{1,0:T(8,128)(2,1)} %param.3) | copy-start | bytes 1572868
  119.4 20.8 %collective-permute-start.15 = (bf16[256,1024]{1,0:T(8,128)(2,1)S(1)}, bf16[256,1024]{1,0:T(8,128)(2,1)S(1)}, u32[]{:S(2)}, u32[]{:S(2)}) collective-permute-start(bf16[256,1024]{1,0:T(8,128)(2,1)S(1)} %collective-permute-done.14), channel_id=1, source_target_pairs={{4,0},{8,4},{12,8},{16,12},{20,16},{24,20},{28,24},{5,1},{9,5},{13... | collective-permute-start | bytes 1572872 | tf_op jit(solution)/shard_map/ppermute | solution.py:15
  145.1 0.7 copy-start.3
  217.7 0.9 copy-start.1
Sparse Core Ops, SparseCore 0:
  145.2 64.3 all-gather.2
